TPU v7x, 128 devices: a whole 4x4x4 slice. The times are simulated.
128 devices in a mesh: px: 8 (over y, core), py: 16 (over z, x).
Axes of the slice: x: 4, y: 4, z: 4, core: 2. Of those that a mesh axis runs over, the one named last changes fastest.
Arguments:
- kappa: bfloat16 [301056, 128], P(('px', 'py')), may hold values from -6 to 6
- send_list: int32 [128, 128, 192], P(('px', 'py')), may hold values from 0 to 2351, as said below
- dest_slot: int32 [128, 128, 192], P(('px', 'py')), may hold values from 0 to 2047, as said below
- send_count: int32 [128, 128], P(('px', 'py')), may hold values from 0 to 192, as said below
Outputs:
- flexion: float32 [4, 4096, 8192], P(None, 'px', 'py')
Inputs may be any that keep to these rules, and one draw needn't show every extreme that they name: For k < send_count[a, d], send_list[a, d, k] is a row of source a's own 2352 tiles; later entries are 0. Over all sources a and k < send_count[a, d], dest_slot[a, d, k] names every slot of patch d exactly once; later entries are 0. send_count[a, d] is nonzero only where d's patch row equals a's px index or is one less; it is a multiple of 4, and reaches 192 in every draw. Summed over the sources a whose px index is one more than d's patch row, it is exactly 512.
All inputs are finite; a program needn't handle non-finite values.
Results may differ from a plain program's by a relative error of at most 0.0065.
Values may be sent and summed in bfloat16 or wider, within the bound.
No kernel may reach another device: no remote copies, remote signals or barrier semaphores. Data moves between devices by JAX's collectives and lax.ppermute only.
A program may use at most 64 MiB of HBM per device.

v0:
```python
import math
import jax
import jax.numpy as jnp
from jax import lax
from jax.sharding import PartitionSpec as P

PATCH_ROWS = 512
PATCH_COLS = 512


def shifted(shard, axis, by):
    size = lax.axis_size(axis)
    pairs = [(i, i + by) for i in range(size) if 0 <= i + by < size]
    return lax.ppermute(shard, axis, pairs)


def padded(block, sides, width):
    for axis, dim in sides:
        count = lax.axis_size(axis)
        forward = [(i, i + 1) for i in range(count - 1)]
        backward = [(target, source) for source, target in forward]
        low = lax.ppermute(
            lax.slice_in_dim(block, block.shape[dim] - width, None, axis=dim), axis, forward
        )
        high = lax.ppermute(lax.slice_in_dim(block, 0, width, axis=dim), axis, backward)
        block = jnp.concatenate([low, block, high], axis=dim)
    return block


def dft_tables(length):
    positions = jnp.arange(length, dtype=jnp.int32)
    phases = positions[:, None] * positions[None, :] % length
    angles = phases.astype(jnp.float32) * (2.0 * math.pi / length)
    return (jnp.cos(angles), jnp.sin(angles))


def wavenumbers(length):
    positions = jnp.arange(length, dtype=jnp.int32)
    signed = positions - length * (positions >= (length + 1) // 2).astype(jnp.int32)
    return signed.astype(jnp.float32) * (2.0 / length)


def flexion_fields(pixels):
    row_count = pixels.shape[0]
    col_count = pixels.shape[1]
    cos_cols, sin_cols = dft_tables(col_count)
    cos_rows, sin_rows = dft_tables(row_count)
    forward_cols = jnp.concatenate([cos_cols, sin_cols], axis=1).astype(jnp.bfloat16)
    halves = jnp.dot(pixels, forward_cols, preferred_element_type=jnp.float32)
    stacked = jnp.concatenate([halves[:, :col_count], halves[:, col_count:]], axis=0).astype(
        jnp.bfloat16
    )
    forward_rows = jnp.concatenate(
        [
            jnp.concatenate([cos_rows, -sin_rows], axis=1),
            jnp.concatenate([-sin_rows, -cos_rows], axis=1),
        ],
        axis=0,
    ).astype(jnp.bfloat16)
    spectrum = jnp.dot(forward_rows, stacked, preferred_element_type=jnp.float32)
    real_part = spectrum[:row_count]
    imag_part = spectrum[row_count:]
    across = wavenumbers(col_count)[None, :]
    down = wavenumbers(row_count)[:, None]
    scale = 1.0 / (row_count * col_count)
    power = across * across + down * down
    safe_power = jnp.where(power > 0, power, 1.0)
    cube_real = across * across * across - 3.0 * across * down * down
    cube_imag = 3.0 * across * across * down - down * down * down
    one_real = (-down * real_part - across * imag_part) * scale
    one_imag = (across * real_part - down * imag_part) * scale
    kernel_real = -cube_imag / safe_power
    kernel_imag = cube_real / safe_power
    three_real = (kernel_real * real_part - kernel_imag * imag_part) * scale
    three_imag = (kernel_real * imag_part + kernel_imag * real_part) * scale
    spectra = jnp.concatenate(
        [
            jnp.concatenate([one_real, three_real], axis=1),
            jnp.concatenate([one_imag, three_imag], axis=1),
        ],
        axis=0,
    ).astype(jnp.bfloat16)
    inverse_rows = jnp.concatenate(
        [
            jnp.concatenate([cos_rows, -sin_rows], axis=1),
            jnp.concatenate([sin_rows, cos_rows], axis=1),
        ],
        axis=0,
    ).astype(jnp.bfloat16)
    columns_done = jnp.dot(inverse_rows, spectra, preferred_element_type=jnp.float32).astype(
        jnp.bfloat16
    )
    arranged = jnp.concatenate(
        [
            jnp.concatenate(
                [columns_done[:row_count, :col_count], columns_done[row_count:, :col_count]], axis=1
            ),
            jnp.concatenate(
                [columns_done[:row_count, col_count:], columns_done[row_count:, col_count:]], axis=1
            ),
        ],
        axis=0,
    )
    inverse_cols = jnp.concatenate(
        [
            jnp.concatenate([cos_cols, sin_cols], axis=1),
            jnp.concatenate([-sin_cols, cos_cols], axis=1),
        ],
        axis=0,
    ).astype(jnp.bfloat16)
    result = jnp.dot(arranged, inverse_cols, preferred_element_type=jnp.float32)
    return jnp.stack(
        [
            result[:row_count, :col_count],
            result[:row_count, col_count:],
            result[row_count:, :col_count],
            result[row_count:, col_count:],
        ]
    ).astype(jnp.bfloat16)


def blend_edges(extended, has_top, has_bottom, has_left, has_right, width):
    values = extended.astype(jnp.float32)
    row_count = values.shape[1] - 2 * width
    col_count = values.shape[2] - 2 * width
    ramp = (jnp.arange(width, dtype=jnp.float32) + 0.5) / width
    top_weight = jnp.where(has_top, ramp, 1.0)[None, :, None]
    bottom_weight = jnp.where(has_bottom, ramp[::-1], 1.0)[None, :, None]
    middle = values[:, width : width + row_count, :]
    top_band = top_weight * middle[:, :width] + (1.0 - top_weight) * values[:, :width]
    bottom_band = (
        bottom_weight * middle[:, row_count - width :]
        + (1.0 - bottom_weight) * values[:, row_count + width :]
    )
    middle = jnp.concatenate([top_band, middle[:, width : row_count - width], bottom_band], axis=1)
    left_weight = jnp.where(has_left, ramp, 1.0)[None, None, :]
    right_weight = jnp.where(has_right, ramp[::-1], 1.0)[None, None, :]
    inner = middle[:, :, width : width + col_count]
    left_band = left_weight * inner[:, :, :width] + (1.0 - left_weight) * middle[:, :, :width]
    right_band = (
        right_weight * inner[:, :, col_count - width :]
        + (1.0 - right_weight) * middle[:, :, col_count + width :]
    )
    return jnp.concatenate([left_band, inner[:, :, width : col_count - width], right_band], axis=2)


def on_device(kappa, send_list, dest_slot, send_count):
    tile_width = kappa.shape[1]
    rows_axis = lax.axis_size("px")
    cols_axis = lax.axis_size("py")
    band_index = lax.axis_index("px")
    column_index = lax.axis_index("py")
    tile_lists = send_list[0].reshape(rows_axis, cols_axis, -1)
    slot_lists = dest_slot[0].reshape(rows_axis, cols_axis, -1)
    pair_counts = send_count[0].reshape(rows_axis, cols_axis)
    slot_depth = tile_lists.shape[2]
    upper_band = jnp.maximum(band_index - 1, 0)
    picked_lists = jnp.stack([tile_lists[band_index], tile_lists[upper_band]], axis=1)
    picked_slots = jnp.stack([slot_lists[band_index], slot_lists[upper_band]], axis=1)
    upper_counts = jnp.where(band_index > 0, pair_counts[upper_band], 0)
    picked_counts = jnp.stack([pair_counts[band_index], upper_counts], axis=1)
    live_mask = jnp.arange(slot_depth, dtype=jnp.int32)[None, None, :] < picked_counts[:, :, None]
    slot_codes = jnp.where(live_mask, picked_slots + 1, 0)
    whole_band, band_lists, band_codes = (
        lax.all_gather(kappa, "py", axis=0, tiled=True),
        lax.all_gather(picked_lists, "py", axis=0, tiled=True),
        lax.all_gather(slot_codes, "py", axis=0, tiled=True),
    )
    own_lists = band_lists.reshape(cols_axis, cols_axis, 2, slot_depth)[:, column_index]
    arrived_codes = band_codes.reshape(cols_axis, cols_axis, 2, slot_depth)[:, column_index]
    offsets = (jnp.arange(cols_axis, dtype=jnp.int32) * kappa.shape[0])[:, None, None]
    tile_values = whole_band[own_lists + offsets]
    raised_values, raised_codes = shifted((tile_values[:, 1], arrived_codes[:, 1]), "px", -1)
    all_values = jnp.concatenate(
        [tile_values[:, 0].reshape(-1, tile_width), raised_values.reshape(-1, tile_width)], axis=0
    )
    all_codes = jnp.concatenate([arrived_codes[:, 0].reshape(-1), raised_codes.reshape(-1)], axis=0)
    slot_total = PATCH_ROWS * PATCH_COLS // tile_width
    target = jnp.where(all_codes > 0, all_codes - 1, slot_total)
    patch_tiles = (
        jnp.zeros((slot_total, tile_width), kappa.dtype).at[target].set(all_values, mode="drop")
    )
    fields = flexion_fields(patch_tiles.reshape(PATCH_ROWS, PATCH_COLS))
    extended = padded(fields, (("px", 1), ("py", 2)), tile_width)
    return blend_edges(
        extended,
        band_index > 0,
        band_index < rows_axis - 1,
        column_index > 0,
        column_index < cols_axis - 1,
        tile_width,
    )


def solution(mesh):
    placed = (
        P(("px", "py"), None),
        P(("px", "py"), None, None),
        P(("px", "py"), None, None),
        P(("px", "py"), None),
    )
    return jax.shard_map(
        on_device, mesh=mesh, in_specs=placed, out_specs=P(None, "px", "py"), check_vma=False
    )
```

profile of v0, /device:TPU:15, one launch (start us, length us, event | category | flops | bytes accessed | tf_op | source)
XLA Modules:
  0.0 213.1 jit_solution(5844957314642020017)
XLA Ops:
  6.5 0.0 all-gather.2.cloned.1.call-start
  6.5 0.7 all-gather.2.cloned.1.call-update
  7.3 0.5 broadcast.420
  7.8 1.3 reduce.3
  9.1 0.1 reshape_squeeze.13
  9.2 1.0 copy.5
  10.2 1.0 copy.6
  11.2 0.1 fusion.57
  11.3 21.8 %all_gather.9 = s32[256,2,192]{2,0,1:T(8,128)S(1)} all-gather(s32[16,2,192]{2,0,1:T(8,128)S(1)} %fusion.57), channel_id=1, replica_groups=mesh['px'=8,'py'=16] {'py'}, dimensions={0}, use_global_device_ids=true | all-gather | bytes 417792 | tf_op jit(solution)/shard_map/all_gather | solution.py:167
  33.1 6.5 %collective-permute-start = (s32[16,192]{1,0:T(8,128)S(1)}, s32[16,192]{1,0:T(8,128)S(1)}, u32[]{:S(2)}, u32[]{:S(2)}) collective-permute-start(s32[16,192]{1,0:T(8,128)S(1)} %get-tuple-element.41), channel_id=1, source_target_pairs={{16,0},{32,16},{48,32},{64,48},{80,64},{96,80},{112,96},{17,1},{33... | collective-permute-start | bytes 36872 | tf_op jit(solution)/shard_map/ppermute | solution.py:14
  39.7 0.1 concatenate.97
  39.8 18.9 %all_gather.11 = s32[256,2,192]{2,0,1:T(8,128)S(1)} all-gather(s32[16,2,192]{2,0,1:T(8,128)S(1)} %pad_add_fusion), channel_id=1, replica_groups=mesh['px'=8,'py'=16] {'py'}, dimensions={0}, use_global_device_ids=true | all-gather | bytes 417792 | tf_op jit(solution)/shard_map/all_gather | solution.py:166
  58.7 0.1 compare_select_fusion.3
  58.8 0.1 reshape.198
  58.9 4.0 %fusion.54 = bf16[512,512]{1,0:T(8,128)(2,1)S(1)} fusion(), kind=kLoop, calls=%fused_computation.93 | loop fusion | flops 4194304 | bytes 524288 | tf_op jit(solution)/shard_map/neg | solution.py:85
  62.9 4.3 %fusion.50 = (bf16[512,512]{1,0:T(8,128)(2,1)S(1)}, bf16[512,512]{1,0:T(8,128)(2,1)S(1)}) fusion(), kind=kLoop, calls=%fused_computation.89 | loop fusion | flops 4194304 | bytes 1048576 | tf_op jit(solution)/shard_map/sin | solution.py:34
  67.3 5.0 %negate_convert_fusion = (bf16[512,512]{1,0:T(8,128)(2,1)}, bf16[512,512]{1,0:T(8,128)(2,1)}) fusion(), kind=kLoop, calls=%fused_computation.70 | loop fusion | flops 4718592 | bytes 1048576 | tf_op jit(solution)/shard_map/convert.29
  72.3 5.0 %fusion.52 = (bf16[512,512]{1,0:T(8,128)(2,1)}, bf16[512,512]{1,0:T(8,128)(2,1)}) fusion(), kind=kLoop, calls=%fused_computation.91 | loop fusion | flops 4194304 | bytes 1048576 | tf_op jit(solution)/shard_map/convert.33
  77.2 1.2 fusion.2
  78.5 0.0 collective-permute-done
  78.5 0.1 concatenate.98
  78.6 12.6 %all-gather.2.cloned.1.call-done = bf16[37632,128]{1,0:T(8,128)(2,1)} async-done(((bf16[2352,128]{1,0:T(8,128)(2,1)}), bf16[37632,128]{1,0:T(8,128)(2,1)}) %all-gather.2.cloned.1.call-update) | async-done | bytes 9633808 | tf_op jit(solution)/shard_map/all_gather | solution.py:165
  91.2 21.4 %gather_fusion = bf16[6144,128]{1,0:T(8,128)(2,1)S(1)} fusion(bf16[37632,128]{1,0:T(8,128)(2,1)} %all-gather.2.cloned.1.call-done, s32[6144]{0:T(1024)S(1)} %broadcast_clamp_fusion), kind=kCustom, calls=%fused_computation | custom fusion | bytes 3170304 | tf_op jit(solution)/shard_map/gather | solution.py:172
  112.7 0.1 fusion.71
  112.8 2.6 %collective-permute-start.1 = (bf16[16,192,128]{2,1,0:T(8,128)(2,1)S(1)}, bf16[16,192,128]{2,1,0:T(8,128)(2,1)S(1)}, u32[]{:S(2)}, u32[]{:S(2)}) collective-permute-start(bf16[16,192,128]{2,1,0:T(8,128)(2,1)S(1)} %get-tuple-element.32), channel_id=1, source_target_pairs={{16,0},{32,16},{48,32},{64,48},{80,64},{96,80},{112,96},{17,1},{33... | collective-permute-start | bytes 2359304 | tf_op jit(solution)/shard_map/ppermute | solution.py:14
  115.5 10.7 %collective-permute-done.1 = bf16[16,192,128]{2,1,0:T(8,128)(2,1)S(1)} collective-permute-done((bf16[16,192,128]{2,1,0:T(8,128)(2,1)S(1)}, bf16[16,192,128]{2,1,0:T(8,128)(2,1)S(1)}, u32[]{:S(2)}, u32[]{:S(2)}) %collective-permute-start.1) | collective-permute-done | bytes 786464 | tf_op jit(solution)/shard_map/ppermute | solution.py:14
  126.2 21.4 %scatter_custom_fusion = bf16[2048,128]{1,0:T(8,128)(2,1)S(1)} fusion(s32[6144]{0:T(1024)S(1)} %bitcast.53, bf16[3072,128]{1,0:T(8,128)(2,1)S(1)} %bitcast.47, bf16[]{:T(256)} %constant.88, bf16[3072,128]{1,0:T(8,128)(2,1)S(1)} %bitcast.46, bf16[]{:T(256)} %constant.24.clone.1), kind=kCustom, calls=%fused_computation.44 | custom fusion | flops 3145728 | bytes 2097156 | tf_op jit(solution)/shard_map/scatter | solution.py:181
  147.5 0.3 reshape.195
  147.9 0.0 copy-start
  147.9 0.0 copy-start.1
  147.9 0.0 copy-start.4
  147.9 0.7 convolution_convert_fusion
  148.6 0.1 fusion.72
  148.7 0.4 copy-done
  149.1 0.1 copy-done.1
  149.2 0.2 copy-done.4
  149.4 1.3 fusion.1
  150.7 0.0 copy-start.2
  150.7 0.0 copy-start.3
  150.7 1.4 multiply_convert_fusion.3
  152.1 0.0 copy-done.2
  152.1 0.0 copy-done.3
  152.1 2.4 %fusion.29 = bf16[1024,1024]{0,1:T(8,128)(2,1)S(1)} fusion(bf16[512,512]{0,1:T(8,128)(2,1)S(1)} %get-tuple-element.19, bf16[512,512]{0,1:T(8,128)(2,1)S(1)} %get-tuple-element.18, bf16[512,512]{0,1:T(8,128)(2,1)S(1)} %get-tuple-element.20, bf16[512,512]{0,1:T(8,128)(2,1)S(1)} %get-tuple-element.17, bf16[512,1024]{1,0:T(8,128)(2,1)S(1)} %copy-done, ...), kind=kOutput, calls=%fused_computation.37 | convolution fusion | flops 2163212288 | bytes 6291456 | tf_op jit(solution)/shard_map/dot_general | solution.py:90
  154.5 0.2 fusion.70
  154.7 2.4 %fusion.24 = bf16[1024,1024]{1,0:T(8,128)(2,1)S(1)} fusion(bf16[512,512]{1,0:T(8,128)(2,1)S(1)} %copy-done.2, bf16[512,512]{1,0:T(8,128)(2,1)S(1)} %copy-done.1, bf16[512,1024]{1,0:T(8,128)(2,1)S(1)} %get-tuple-element.36, bf16[512,512]{0,1:T(8,128)(2,1)S(1)} %get-tuple-element.28, bf16[512,512]{0,1:T(8,128)(2,1)S(1)} %get-tuple-element.29, ...), kind=kOutput, calls=%fused_computation.36 | convolution fusion | flops 2163212288 | bytes 6291456 | tf_op jit(solution)/shard_map/dot_general | solution.py:111
  157.1 0.2 slice_bitcast_fusion.4
  157.3 0.1 pad_maximum_fusion.24
  157.4 1.9 collective-permute-start.2
  159.3 2.4 %collective-permute-start.3 = (bf16[4,128,512]{2,1,0:T(8,128)(2,1)S(1)}, bf16[4,128,512]{2,1,0:T(8,128)(2,1)S(1)}, u32[]{:S(2)}, u32[]{:S(2)}) collective-permute-start(bf16[4,128,512]{2,1,0:T(8,128)(2,1)S(1)} %get-tuple-element.22), channel_id=1, source_target_pairs={{16,0},{32,16},{48,32},{64,48},{80,64},{96,80},{112,96},{17,1},{33... | collective-permute-start | bytes 1572872 | tf_op jit(solution)/shard_map/ppermute | solution.py:25
  161.7 3.7 %collective-permute-done.2 = bf16[4,128,512]{2,1,0:T(8,128)(2,1)S(1)} collective-permute-done((bf16[4,128,512]{2,1,0:T(8,128)(2,1)S(1)}, bf16[4,128,512]{2,1,0:T(8,128)(2,1)S(1)}, u32[]{:S(2)}, u32[]{:S(2)}) %collective-permute-start.2) | collective-permute-done | bytes 524320 | tf_op jit(solution)/shard_map/ppermute | solution.py:22
  165.4 4.4 %collective-permute-done.3 = bf16[4,128,512]{2,1,0:T(8,128)(2,1)S(1)} collective-permute-done((bf16[4,128,512]{2,1,0:T(8,128)(2,1)S(1)}, bf16[4,128,512]{2,1,0:T(8,128)(2,1)S(1)}, u32[]{:S(2)}, u32[]{:S(2)}) %collective-permute-start.3) | collective-permute-done | bytes 524320 | tf_op jit(solution)/shard_map/ppermute | solution.py:25
  169.8 1.5 pad_maximum_fusion.20
  171.3 3.0 %collective-permute-start.4 = (bf16[4,768,128]{2,1,0:T(8,128)(2,1)}, bf16[4,768,128]{2,1,0:T(8,128)(2,1)}, u32[]{:S(2)}, u32[]{:S(2)}) collective-permute-start(bf16[4,768,128]{2,1,0:T(8,128)(2,1)} %get-tuple-element.13), channel_id=1, source_target_pairs={{0,1},{1,2},{2,3},{3,4},{4,5},{5,6},{6,7},{7,8},{8,9},{9,10},{10,1... | collective-permute-start | bytes 2359304 | tf_op jit(solution)/shard_map/ppermute | solution.py:22
  174.3 2.3 %collective-permute-start.5 = (bf16[4,768,128]{2,1,0:T(8,128)(2,1)}, bf16[4,768,128]{2,1,0:T(8,128)(2,1)}, u32[]{:S(2)}, u32[]{:S(2)}) collective-permute-start(bf16[4,768,128]{2,1,0:T(8,128)(2,1)} %get-tuple-element.14), channel_id=1, source_target_pairs={{1,0},{2,1},{3,2},{4,3},{5,4},{6,5},{7,6},{8,7},{9,8},{10,9},{11,1... | collective-permute-start | bytes 2359304 | tf_op jit(solution)/shard_map/ppermute | solution.py:25
  176.6 0.1 reverse.4
  176.7 15.5 %collective-permute-done.4 = bf16[4,768,128]{2,1,0:T(8,128)(2,1)} collective-permute-done((bf16[4,768,128]{2,1,0:T(8,128)(2,1)}, bf16[4,768,128]{2,1,0:T(8,128)(2,1)}, u32[]{:S(2)}, u32[]{:S(2)}) %collective-permute-start.4) | collective-permute-done | bytes 786464 | tf_op jit(solution)/shard_map/ppermute | solution.py:22
  192.2 5.2 %collective-permute-done.5 = bf16[4,768,128]{2,1,0:T(8,128)(2,1)} collective-permute-done((bf16[4,768,128]{2,1,0:T(8,128)(2,1)}, bf16[4,768,128]{2,1,0:T(8,128)(2,1)}, u32[]{:S(2)}, u32[]{:S(2)}) %collective-permute-start.5) | collective-permute-done | bytes 786464 | tf_op jit(solution)/shard_map/ppermute | solution.py:25
  197.4 4.6 %maximum_convert_fusion = f32[4,768,768]{2,1,0:T(8,128)S(1)} fusion(bf16[4,768,128]{2,1,0:T(8,128)(2,1)} %collective-permute-done.5, bf16[4,128,512]{2,1,0:T(8,128)(2,1)S(1)} %collective-permute-done.3, bf16[1,512,512]{2,1,0:T(8,128)(2,1)S(1)} %get-tuple-element.24, bf16[1,512,512]{2,1,0:T(8,128)(2,1)S(1)} %get-tuple-element.25, ...), kind=kLoop, calls=%fused_computation.3 | loop fusion | flops 37748736 | bytes 14155776 | tf_op jit(solution)/shard_map/convert_element_type | solution.py:123
  202.0 0.2 slice.154
  202.2 0.5 fusion.33
  202.7 0.6 pad_maximum_fusion
  203.3 0.1 slice.157
  203.5 0.2 fusion.42
  203.7 2.5 %pad_maximum_fusion.1 = f32[4,512,512]{2,1,0:T(8,128)} fusion(f32[4,512,128]{2,1,0:T(8,128)S(1)} %get-tuple-element.12, f32[4,512,256]{2,1,0:T(8,128)S(1)} %slice.157, f32[4,512,128]{2,1,0:T(8,128)S(1)} %get-tuple-element.11), kind=kLoop, calls=%fused_computation.4 | loop fusion | flops 2097152 | bytes 8388608 | tf_op jit(solution)/shard_map/concatenate | solution.py:144
  (21 shorter events, 0.3 us)
Async XLA Ops:
  6.5 84.7 %all-gather.2.cloned.1.call-start = ((), (), s32[]{:S(2)}) async-start(), calls=%async_computation | async-start | bytes 10235904 | tf_op jit(solution)/shard_map/all_gather | solution.py:165
  33.1 45.4 %collective-permute-start = (s32[16,192]{1,0:T(8,128)S(1)}, s32[16,192]{1,0:T(8,128)S(1)}, u32[]{:S(2)}, u32[]{:S(2)}) collective-permute-start(s32[16,192]{1,0:T(8,128)S(1)} %get-tuple-element.41), channel_id=1, source_target_pairs={{16,0},{32,16},{48,32},{64,48},{80,64},{96,80},{112,96},{17,1},{33... | collective-permute-start | bytes 36872 | tf_op jit(solution)/shard_map/ppermute | solution.py:14
  112.8 13.4 %collective-permute-start.1 = (bf16[16,192,128]{2,1,0:T(8,128)(2,1)S(1)}, bf16[16,192,128]{2,1,0:T(8,128)(2,1)S(1)}, u32[]{:S(2)}, u32[]{:S(2)}) collective-permute-start(bf16[16,192,128]{2,1,0:T(8,128)(2,1)S(1)} %get-tuple-element.32), channel_id=1, source_target_pairs={{16,0},{32,16},{48,32},{64,48},{80,64},{96,80},{112,96},{17,1},{33... | collective-permute-start | bytes 2359304 | tf_op jit(solution)/shard_map/ppermute | solution.py:14
  147.9 1.2 copy-start
  147.9 1.3 copy-start.1
  147.9 1.5 copy-start.4
  150.7 1.4 copy-start.2
  150.7 1.4 copy-start.3
  157.4 8.0 %collective-permute-start.2 = (bf16[4,128,512]{2,1,0:T(8,128)(2,1)S(1)}, bf16[4,128,512]{2,1,0:T(8,128)(2,1)S(1)}, u32[]{:S(2)}, u32[]{:S(2)}) collective-permute-start(bf16[4,128,512]{2,1,0:T(8,128)(2,1)S(1)} %get-tuple-element.21), channel_id=1, source_target_pairs={{0,16},{16,32},{32,48},{48,64},{64,80},{80,96},{96,112},{1,17},{17... | collective-permute-start | bytes 1572872 | tf_op jit(solution)/shard_map/ppermute | solution.py:22
  159.3 10.5 %collective-permute-start.3 = (bf16[4,128,512]{2,1,0:T(8,128)(2,1)S(1)}, bf16[4,128,512]{2,1,0:T(8,128)(2,1)S(1)}, u32[]{:S(2)}, u32[]{:S(2)}) collective-permute-start(bf16[4,128,512]{2,1,0:T(8,128)(2,1)S(1)} %get-tuple-element.22), channel_id=1, source_target_pairs={{16,0},{32,16},{48,32},{64,48},{80,64},{96,80},{112,96},{17,1},{33... | collective-permute-start | bytes 1572872 | tf_op jit(solution)/shard_map/ppermute | solution.py:25
  171.3 21.0 %collective-permute-start.4 = (bf16[4,768,128]{2,1,0:T(8,128)(2,1)}, bf16[4,768,128]{2,1,0:T(8,128)(2,1)}, u32[]{:S(2)}, u32[]{:S(2)}) collective-permute-start(bf16[4,768,128]{2,1,0:T(8,128)(2,1)} %get-tuple-element.13), channel_id=1, source_target_pairs={{0,1},{1,2},{2,3},{3,4},{4,5},{5,6},{6,7},{7,8},{8,9},{9,10},{10,1... | collective-permute-start | bytes 2359304 | tf_op jit(solution)/shard_map/ppermute | solution.py:22
  174.3 23.1 %collective-permute-start.5 = (bf16[4,768,128]{2,1,0:T(8,128)(2,1)}, bf16[4,768,128]{2,1,0:T(8,128)(2,1)}, u32[]{:S(2)}, u32[]{:S(2)}) collective-permute-start(bf16[4,768,128]{2,1,0:T(8,128)(2,1)} %get-tuple-element.14), channel_id=1, source_target_pairs={{1,0},{2,1},{3,2},{4,3},{5,4},{6,5},{7,6},{8,7},{9,8},{10,9},{11,1... | collective-permute-start | bytes 2359304 | tf_op jit(solution)/shard_map/ppermute | solution.py:25
Sparse Core Ops, SparseCore 0:
  9.5 81.6 all-gather.1
where the time goes:
time: 214 us; the launch traced here: 213 us
  other arithmetic  53.8 us (25%)
  waiting for transfers between devices  52.8 us (25%)
  blocking collectives  40.7 us (19%)
  local copies, waits for them, and re-layouts  26.4 us (12%)
  starting transfers between devices  18.7 us (9%)
  between operations  13.8 us (6%)
  matrix products  6.84 us (3%)
    all_gather x1, blocking collectives, on_device(): lax.all_gather(slot_codes, 'py', axis=0, tiled=True)  21.8 us
    gather x1, local copies, waits for them, and re-layouts, on_device(): tile_values = whole_band[own_lists + offsets]  21.4 us
    scatter x1, other arithmetic, on_device(): jnp.zeros((slot_total, tile_width), kappa.dtype).at[target]  21.4 us
    ppermute x2, waiting for transfers between devices, padded(): lax.ppermute(lax.slice_in_dim(block, block.shape[dim] - width, None, axis...  19.2 us
    all_gather x1, blocking collectives, on_device(): lax.all_gather(picked_lists, 'py', axis=0, tiled=True)  18.9 us
    all_gather x1, waiting for transfers between devices, on_device(): lax.all_gather(kappa, 'py', axis=0, tiled=True)  12.6 us
    another operation x4, other arithmetic  12.6 us
    ppermute x2, waiting for transfers between devices, shifted(): return lax.ppermute(shard, axis, pairs)  10.7 us
  transfers between devices with their start and end apart: 7, of which 6 were waited for; matrix products, arithmetic and copies ran while one was open for 11% of the time, Pallas kernels for 0%

commit v1 on v0

--- a/solution.py
+++ b/solution.py
@@ -6,6 +6,22 @@
 
 PATCH_ROWS = 512
 PATCH_COLS = 512
+
+
+def ring_gather(x, axis, dim):
+    ways, here, step = (lax.axis_size(axis), lax.axis_index(axis), x.shape[dim])
+    dims = [n * ways if d == dim else n for d, n in enumerate(x.shape)]
+    full = lax.dynamic_update_slice_in_dim(jnp.zeros(dims, x.dtype), x, here * step, axis=dim)
+    going_up = going_down = x
+    for far in range(1, ways // 2 + 1):
+        going_up = lax.ppermute(going_up, axis, [(d, (d + 1) % ways) for d in range(ways)])
+        full = lax.dynamic_update_slice_in_dim(full, going_up, (here - far) % ways * step, axis=dim)
+        if 2 * far < ways:
+            going_down = lax.ppermute(going_down, axis, [(d, (d - 1) % ways) for d in range(ways)])
+            full = lax.dynamic_update_slice_in_dim(
+                full, going_down, (here + far) % ways * step, axis=dim
+            )
+    return full
 
 
 def shifted(shard, axis, by):
@@ -163,7 +179,7 @@
     slot_codes = jnp.where(live_mask, picked_slots + 1, 0)
     whole_band, band_lists, band_codes = (
         lax.all_gather(kappa, "py", axis=0, tiled=True),
-        lax.all_gather(picked_lists, "py", axis=0, tiled=True),
+        ring_gather(picked_lists, "py", 0),
         lax.all_gather(slot_codes, "py", axis=0, tiled=True),
     )
     own_lists = band_lists.reshape(cols_axis, cols_axis, 2, slot_depth)[:, column_index]

time: 214 us -> 235 us (1.098)
  the two profiles are of different devices: /device:TPU:15 before, /device:TPU:17 now
where the time goes in v1:
time: 235 us
  starting transfers between devices  58.9 us (25%)
  waiting for transfers between devices  55.5 us (24%)
  other arithmetic  53.6 us (23%)
  local copies, waits for them, and re-layouts  26.5 us (11%)
  blocking collectives  19.5 us (8%)
  between operations  13.9 us (6%)
  matrix products  6.83 us (3%)
    ppermute x7, starting transfers between devices, ring_gather(): lax.ppermute(going_down, axis, [(d, (d - 1) % ways) for d in range(ways)])  33.5 us
    gather x1, local copies, waits for them, and re-layouts, on_device(): tile_values = whole_band[own_lists + offsets]  21.4 us
    scatter x1, other arithmetic, on_device(): jnp.zeros((slot_total, tile_width), kappa.dtype).at[target]  21.2 us
    all_gather x1, blocking collectives, on_device(): lax.all_gather(slot_codes, 'py', axis=0, tiled=True)  19.5 us
    ppermute x2, waiting for transfers between devices, padded(): lax.ppermute(lax.slice_in_dim(block, block.shape[dim] - width, None, axis...  17.9 us
    ppermute x8, waiting for transfers between devices, ring_gather(): lax.ppermute(going_up, axis, [(d, (d + 1) % ways) for d in range(ways)])  16.9 us
    ppermute x2, starting transfers between devices, shifted(): return lax.ppermute(shard, axis, pairs)  16 us
    another operation x4, other arithmetic  12.6 us
  transfers between devices with their start and end apart: 22, of which 12 were waited for; matrix products, arithmetic and copies ran while one was open for 10% of the time, Pallas kernels for 0%

profile of v1, /device:TPU:17, one launch (start us, length us, event | category | flops | bytes accessed | tf_op | source)
XLA Modules:
  0.0 234.7 jit_solution(13334318457364611865)
XLA Ops:
  6.5 0.7 all-gather.2.cloned.1.call-update
  7.3 1.0 copy.5
  8.3 1.0 copy.6
  9.3 1.3 collective-permute-start.1
  10.6 4.8 %collective-permute-start.2 = (s32[16,2,192]{2,0,1:T(8,128)S(1)}, s32[16,2,192]{2,0,1:T(8,128)S(1)}, u32[]{:S(2)}, u32[]{:S(2)}) collective-permute-start(s32[16,2,192]{2,0,1:T(8,128)S(1)} %get-tuple-element.41), channel_id=1, source_target_pairs={{0,15},{1,0},{2,1},{3,2},{4,3},{5,4},{6,5},{7,6},{8,7},{9,8},{10,9... | collective-permute-start | bytes 73736 | tf_op jit(solution)/shard_map/ppermute | solution.py:20
  15.4 0.5 broadcast.435
  16.0 1.3 reduce.3
  17.5 19.5 %all_gather.6 = s32[256,2,192]{2,0,1:T(8,128)S(1)} all-gather(s32[16,2,192]{2,0,1:T(8,128)S(1)} %fusion.57), channel_id=1, replica_groups=mesh['px'=8,'py'=16] {'py'}, dimensions={0}, use_global_device_ids=true | all-gather | bytes 417792 | tf_op jit(solution)/shard_map/all_gather | solution.py:183
  37.0 7.0 %collective-permute-start = (s32[16,192]{1,0:T(8,128)S(1)}, s32[16,192]{1,0:T(8,128)S(1)}, u32[]{:S(2)}, u32[]{:S(2)}) collective-permute-start(s32[16,192]{1,0:T(8,128)S(1)} %get-tuple-element.43), channel_id=1, source_target_pairs={{16,0},{32,16},{48,32},{64,48},{80,64},{96,80},{112,96},{17,1},{33... | collective-permute-start | bytes 36872 | tf_op jit(solution)/shard_map/ppermute | solution.py:30
  44.0 0.1 concatenate.97
  44.1 4.0 %fusion.54 = bf16[512,512]{1,0:T(8,128)(2,1)S(1)} fusion(), kind=kLoop, calls=%fused_computation.93 | loop fusion | flops 4194304 | bytes 524288 | tf_op jit(solution)/shard_map/neg | solution.py:101
  48.1 4.3 %fusion.50 = (bf16[512,512]{1,0:T(8,128)(2,1)S(1)}, bf16[512,512]{1,0:T(8,128)(2,1)S(1)}) fusion(), kind=kLoop, calls=%fused_computation.89 | loop fusion | flops 4194304 | bytes 1048576 | tf_op jit(solution)/shard_map/sin | solution.py:50
  52.5 5.0 %negate_convert_fusion = (bf16[512,512]{1,0:T(8,128)(2,1)}, bf16[512,512]{1,0:T(8,128)(2,1)}) fusion(), kind=kLoop, calls=%fused_computation.70 | loop fusion | flops 4718592 | bytes 1048576 | tf_op jit(solution)/shard_map/convert.29
  57.5 5.0 %fusion.52 = (bf16[512,512]{1,0:T(8,128)(2,1)}, bf16[512,512]{1,0:T(8,128)(2,1)}) fusion(), kind=kLoop, calls=%fused_computation.91 | loop fusion | flops 4194304 | bytes 1048576 | tf_op jit(solution)/shard_map/convert.33
  62.4 1.2 fusion.2
  63.7 0.1 concatenate.98
  63.8 0.1 collective-permute-start.3
  63.9 4.8 %collective-permute-start.4 = (s32[16,2,192]{2,0,1:T(8,128)S(1)}, s32[16,2,192]{2,0,1:T(8,128)S(1)}, u32[]{:S(2)}, u32[]{:S(2)}) collective-permute-start(s32[16,2,192]{2,0,1:T(8,128)S(1)} %collective-permute-done.2), channel_id=1, source_target_pairs={{0,15},{1,0},{2,1},{3,2},{4,3},{5,4},{6,5},{7,6},{8,7},{9,8},{10,9... | collective-permute-start | bytes 73736 | tf_op jit(solution)/shard_map/ppermute | solution.py:20
  68.6 2.4 %collective-permute-done.3 = s32[16,2,192]{2,0,1:T(8,128)S(1)} collective-permute-done((s32[16,2,192]{2,0,1:T(8,128)S(1)}, s32[16,2,192]{2,0,1:T(8,128)S(1)}, u32[]{:S(2)}, u32[]{:S(2)}) %collective-permute-start.3) | collective-permute-done | bytes 24608 | tf_op jit(solution)/shard_map/ppermute | solution.py:17
  71.1 4.8 %collective-permute-start.6 = (s32[16,2,192]{2,0,1:T(8,128)S(1)}, s32[16,2,192]{2,0,1:T(8,128)S(1)}, u32[]{:S(2)}, u32[]{:S(2)}) collective-permute-start(s32[16,2,192]{2,0,1:T(8,128)S(1)} %collective-permute-done.4), channel_id=1, source_target_pairs={{0,15},{1,0},{2,1},{3,2},{4,3},{5,4},{6,5},{7,6},{8,7},{9,8},{10,9... | collective-permute-start | bytes 73736 | tf_op jit(solution)/shard_map/ppermute | solution.py:20
  75.9 2.0 collective-permute-done.5
  77.9 4.8 %collective-permute-start.8 = (s32[16,2,192]{2,0,1:T(8,128)S(1)}, s32[16,2,192]{2,0,1:T(8,128)S(1)}, u32[]{:S(2)}, u32[]{:S(2)}) collective-permute-start(s32[16,2,192]{2,0,1:T(8,128)S(1)} %collective-permute-done.6), channel_id=1, source_target_pairs={{0,15},{1,0},{2,1},{3,2},{4,3},{5,4},{6,5},{7,6},{8,7},{9,8},{10,9... | collective-permute-start | bytes 73736 | tf_op jit(solution)/shard_map/ppermute | solution.py:20
  82.7 2.0 collective-permute-done.7
  84.6 4.8 %collective-permute-start.10 = (s32[16,2,192]{2,0,1:T(8,128)S(1)}, s32[16,2,192]{2,0,1:T(8,128)S(1)}, u32[]{:S(2)}, u32[]{:S(2)}) collective-permute-start(s32[16,2,192]{2,0,1:T(8,128)S(1)} %collective-permute-done.8), channel_id=1, source_target_pairs={{0,15},{1,0},{2,1},{3,2},{4,3},{5,4},{6,5},{7,6},{8,7},{9,8},{10,9... | collective-permute-start | bytes 73736 | tf_op jit(solution)/shard_map/ppermute | solution.py:20
  89.4 1.9 collective-permute-done.9
  91.4 4.8 %collective-permute-start.12 = (s32[16,2,192]{2,0,1:T(8,128)S(1)}, s32[16,2,192]{2,0,1:T(8,128)S(1)}, u32[]{:S(2)}, u32[]{:S(2)}) collective-permute-start(s32[16,2,192]{2,0,1:T(8,128)S(1)} %collective-permute-done.10), channel_id=1, source_target_pairs={{0,15},{1,0},{2,1},{3,2},{4,3},{5,4},{6,5},{7,6},{8,7},{9,8},{10,9... | collective-permute-start | bytes 73736 | tf_op jit(solution)/shard_map/ppermute | solution.py:20
  96.2 1.3 collective-permute-done.11
  97.5 4.8 %collective-permute-start.14 = (s32[16,2,192]{2,0,1:T(8,128)S(1)}, s32[16,2,192]{2,0,1:T(8,128)S(1)}, u32[]{:S(2)}, u32[]{:S(2)}) collective-permute-start(s32[16,2,192]{2,0,1:T(8,128)S(1)} %collective-permute-done.12), channel_id=1, source_target_pairs={{0,15},{1,0},{2,1},{3,2},{4,3},{5,4},{6,5},{7,6},{8,7},{9,8},{10,9... | collective-permute-start | bytes 73736 | tf_op jit(solution)/shard_map/ppermute | solution.py:20
  102.3 1.3 collective-permute-done.13
  103.6 6.0 %collective-permute-done.15 = s32[16,2,192]{2,0,1:T(8,128)S(1)} collective-permute-done((s32[16,2,192]{2,0,1:T(8,128)S(1)}, s32[16,2,192]{2,0,1:T(8,128)S(1)}, u32[]{:S(2)}, u32[]{:S(2)}) %collective-permute-start.15) | collective-permute-done | bytes 24608 | tf_op jit(solution)/shard_map/ppermute | solution.py:17
  109.8 0.1 reshape.198
  109.9 21.4 %gather_fusion = bf16[6144,128]{1,0:T(8,128)(2,1)S(1)} fusion(bf16[37632,128]{1,0:T(8,128)(2,1)} %all-gather.2.cloned.1.call-done, s32[6144]{0:T(1024)S(1)} %broadcast_clamp_fusion), kind=kCustom, calls=%fused_computation | custom fusion | bytes 3170304 | tf_op jit(solution)/shard_map/gather | solution.py:188
  131.3 0.1 fusion.71
  131.5 9.0 %collective-permute-start.16 = (bf16[16,192,128]{2,1,0:T(8,128)(2,1)S(1)}, bf16[16,192,128]{2,1,0:T(8,128)(2,1)S(1)}, u32[]{:S(2)}, u32[]{:S(2)}) collective-permute-start(bf16[16,192,128]{2,1,0:T(8,128)(2,1)S(1)} %get-tuple-element.32), channel_id=1, source_target_pairs={{16,0},{32,16},{48,32},{64,48},{80,64},{96,80},{112,96},{17,1},{33... | collective-permute-start | bytes 2359304 | tf_op jit(solution)/shard_map/ppermute | solution.py:30
  140.5 10.5 %collective-permute-done.16 = bf16[16,192,128]{2,1,0:T(8,128)(2,1)S(1)} collective-permute-done((bf16[16,192,128]{2,1,0:T(8,128)(2,1)S(1)}, bf16[16,192,128]{2,1,0:T(8,128)(2,1)S(1)}, u32[]{:S(2)}, u32[]{:S(2)}) %collective-permute-start.16) | collective-permute-done | bytes 786464 | tf_op jit(solution)/shard_map/ppermute | solution.py:30
  151.0 21.2 %scatter_custom_fusion = bf16[2048,128]{1,0:T(8,128)(2,1)S(1)} fusion(s32[6144]{0:T(1024)S(1)} %bitcast.53, bf16[3072,128]{1,0:T(8,128)(2,1)S(1)} %bitcast.47, bf16[]{:T(256)} %constant.180, bf16[3072,128]{1,0:T(8,128)(2,1)S(1)} %bitcast.46, bf16[]{:T(256)} %constant.147.clone.1), kind=kCustom, calls=%fused_computation.44 | custom fusion | flops 3145728 | bytes 2097156 | tf_op jit(solution)/shard_map/scatter | solution.py:197
  172.2 0.3 reshape.195
  172.6 0.7 convolution_convert_fusion
  173.4 0.4 copy-done
  173.8 0.1 copy-done.1
  173.9 0.2 copy-done.4
  174.1 1.3 fusion.1
  175.4 1.4 multiply_convert_fusion.3
  176.8 2.4 %fusion.29 = bf16[1024,1024]{0,1:T(8,128)(2,1)S(1)} fusion(bf16[512,512]{0,1:T(8,128)(2,1)S(1)} %get-tuple-element.19, bf16[512,512]{0,1:T(8,128)(2,1)S(1)} %get-tuple-element.18, bf16[512,512]{0,1:T(8,128)(2,1)S(1)} %get-tuple-element.20, bf16[512,512]{0,1:T(8,128)(2,1)S(1)} %get-tuple-element.17, bf16[512,1024]{1,0:T(8,128)(2,1)S(1)} %copy-done, ...), kind=kOutput, calls=%fused_computation.37 | convolution fusion | flops 2163212288 | bytes 6291456 | tf_op jit(solution)/shard_map/dot_general | solution.py:106
  179.2 0.2 fusion.70
  179.4 2.4 %fusion.24 = bf16[1024,1024]{1,0:T(8,128)(2,1)S(1)} fusion(bf16[512,512]{1,0:T(8,128)(2,1)S(1)} %copy-done.2, bf16[512,512]{1,0:T(8,128)(2,1)S(1)} %copy-done.1, bf16[512,1024]{1,0:T(8,128)(2,1)S(1)} %get-tuple-element.36, bf16[512,512]{0,1:T(8,128)(2,1)S(1)} %get-tuple-element.28, bf16[512,512]{0,1:T(8,128)(2,1)S(1)} %get-tuple-element.29, ...), kind=kOutput, calls=%fused_computation.36 | convolution fusion | flops 2163212288 | bytes 6291456 | tf_op jit(solution)/shard_map/dot_general | solution.py:127
  181.8 0.2 slice_bitcast_fusion.4
  182.0 1.9 collective-permute-start.17
  184.0 2.4 %collective-permute-start.18 = (bf16[4,128,512]{2,1,0:T(8,128)(2,1)S(1)}, bf16[4,128,512]{2,1,0:T(8,128)(2,1)S(1)}, u32[]{:S(2)}, u32[]{:S(2)}) collective-permute-start(bf16[4,128,512]{2,1,0:T(8,128)(2,1)S(1)} %get-tuple-element.22), channel_id=1, source_target_pairs={{16,0},{32,16},{48,32},{64,48},{80,64},{96,80},{112,96},{17,1},{33... | collective-permute-start | bytes 1572872 | tf_op jit(solution)/shard_map/ppermute | solution.py:41
  186.4 3.7 %collective-permute-done.17 = bf16[4,128,512]{2,1,0:T(8,128)(2,1)S(1)} collective-permute-done((bf16[4,128,512]{2,1,0:T(8,128)(2,1)S(1)}, bf16[4,128,512]{2,1,0:T(8,128)(2,1)S(1)}, u32[]{:S(2)}, u32[]{:S(2)}) %collective-permute-start.17) | collective-permute-done | bytes 524320 | tf_op jit(solution)/shard_map/ppermute | solution.py:38
  190.1 4.4 %collective-permute-done.18 = bf16[4,128,512]{2,1,0:T(8,128)(2,1)S(1)} collective-permute-done((bf16[4,128,512]{2,1,0:T(8,128)(2,1)S(1)}, bf16[4,128,512]{2,1,0:T(8,128)(2,1)S(1)}, u32[]{:S(2)}, u32[]{:S(2)}) %collective-permute-start.18) | collective-permute-done | bytes 524320 | tf_op jit(solution)/shard_map/ppermute | solution.py:41
  194.5 1.5 pad_maximum_fusion.20
  196.0 2.2 collective-permute-start.19
  198.1 1.5 collective-permute-start.20
  199.7 0.1 reverse.4
  199.8 14.2 %collective-permute-done.19 = bf16[4,768,128]{2,1,0:T(8,128)(2,1)} collective-permute-done((bf16[4,768,128]{2,1,0:T(8,128)(2,1)}, bf16[4,768,128]{2,1,0:T(8,128)(2,1)}, u32[]{:S(2)}, u32[]{:S(2)}) %collective-permute-start.19) | collective-permute-done | bytes 786464 | tf_op jit(solution)/shard_map/ppermute | solution.py:38
  214.0 5.0 %collective-permute-done.20 = bf16[4,768,128]{2,1,0:T(8,128)(2,1)} collective-permute-done((bf16[4,768,128]{2,1,0:T(8,128)(2,1)}, bf16[4,768,128]{2,1,0:T(8,128)(2,1)}, u32[]{:S(2)}, u32[]{:S(2)}) %collective-permute-start.20) | collective-permute-done | bytes 786464 | tf_op jit(solution)/shard_map/ppermute | solution.py:41
  219.0 4.6 %maximum_convert_fusion = f32[4,768,768]{2,1,0:T(8,128)S(1)} fusion(bf16[4,768,128]{2,1,0:T(8,128)(2,1)} %collective-permute-done.20, bf16[4,128,512]{2,1,0:T(8,128)(2,1)S(1)} %collective-permute-done.18, bf16[1,512,512]{2,1,0:T(8,128)(2,1)S(1)} %get-tuple-element.24, bf16[1,512,512]{2,1,0:T(8,128)(2,1)S(1)} %get-tuple-element.25, ...), kind=kLoop, calls=%fused_computation.3 | loop fusion | flops 37748736 | bytes 14155776 | tf_op jit(solution)/shard_map/convert_element_type | solution.py:139
  223.6 0.2 slice.154
  223.8 0.5 fusion.33
  224.3 0.6 pad_maximum_fusion
  224.9 0.1 slice.157
  225.1 0.2 fusion.42
  225.3 2.5 %pad_maximum_fusion.1 = f32[4,512,512]{2,1,0:T(8,128)} fusion(f32[4,512,128]{2,1,0:T(8,128)S(1)} %get-tuple-element.12, f32[4,512,256]{2,1,0:T(8,128)S(1)} %slice.157, f32[4,512,128]{2,1,0:T(8,128)S(1)} %get-tuple-element.11), kind=kLoop, calls=%fused_computation.4 | loop fusion | flops 2097152 | bytes 8388608 | tf_op jit(solution)/shard_map/concatenate | solution.py:160
  (66 shorter events, 0.8 us)
Async XLA Ops:
  6.5 103.4 %all-gather.2.cloned.1.call-start = ((), (), s32[]{:S(2)}) async-start(), calls=%async_computation | async-start | bytes 10235904 | tf_op jit(solution)/shard_map/all_gather | solution.py:181
  9.3 54.4 %collective-permute-start.1 = (s32[16,2,192]{2,0,1:T(8,128)S(1)}, s32[16,2,192]{2,0,1:T(8,128)S(1)}, u32[]{:S(2)}, u32[]{:S(2)}) collective-permute-start(s32[16,2,192]{2,0,1:T(8,128)S(1)} %get-tuple-element.41), channel_id=1, source_target_pairs={{0,1},{1,2},{2,3},{3,4},{4,5},{5,6},{6,7},{7,8},{8,9},{9,10},{10,1... | collective-permute-start | bytes 73736 | tf_op jit(solution)/shard_map/ppermute | solution.py:17
  10.6 53.2 %collective-permute-start.2 = (s32[16,2,192]{2,0,1:T(8,128)S(1)}, s32[16,2,192]{2,0,1:T(8,128)S(1)}, u32[]{:S(2)}, u32[]{:S(2)}) collective-permute-start(s32[16,2,192]{2,0,1:T(8,128)S(1)} %get-tuple-element.41), channel_id=1, source_target_pairs={{0,15},{1,0},{2,1},{3,2},{4,3},{5,4},{6,5},{7,6},{8,7},{9,8},{10,9... | collective-permute-start | bytes 73736 | tf_op jit(solution)/shard_map/ppermute | solution.py:20
  37.0 26.7 %collective-permute-start = (s32[16,192]{1,0:T(8,128)S(1)}, s32[16,192]{1,0:T(8,128)S(1)}, u32[]{:S(2)}, u32[]{:S(2)}) collective-permute-start(s32[16,192]{1,0:T(8,128)S(1)} %get-tuple-element.43), channel_id=1, source_target_pairs={{16,0},{32,16},{48,32},{64,48},{80,64},{96,80},{112,96},{17,1},{33... | collective-permute-start | bytes 36872 | tf_op jit(solution)/shard_map/ppermute | solution.py:30
  63.8 7.3 %collective-permute-start.3 = (s32[16,2,192]{2,0,1:T(8,128)S(1)}, s32[16,2,192]{2,0,1:T(8,128)S(1)}, u32[]{:S(2)}, u32[]{:S(2)}) collective-permute-start(s32[16,2,192]{2,0,1:T(8,128)S(1)} %collective-permute-done.1), channel_id=1, source_target_pairs={{0,1},{1,2},{2,3},{3,4},{4,5},{5,6},{6,7},{7,8},{8,9},{9,10},{10,1... | collective-permute-start | bytes 73736 | tf_op jit(solution)/shard_map/ppermute | solution.py:17
  63.9 7.2 %collective-permute-start.4 = (s32[16,2,192]{2,0,1:T(8,128)S(1)}, s32[16,2,192]{2,0,1:T(8,128)S(1)}, u32[]{:S(2)}, u32[]{:S(2)}) collective-permute-start(s32[16,2,192]{2,0,1:T(8,128)S(1)} %collective-permute-done.2), channel_id=1, source_target_pairs={{0,15},{1,0},{2,1},{3,2},{4,3},{5,4},{6,5},{7,6},{8,7},{9,8},{10,9... | collective-permute-start | bytes 73736 | tf_op jit(solution)/shard_map/ppermute | solution.py:20
  71.1 6.8 %collective-permute-start.5 = (s32[16,2,192]{2,0,1:T(8,128)S(1)}, s32[16,2,192]{2,0,1:T(8,128)S(1)}, u32[]{:S(2)}, u32[]{:S(2)}) collective-permute-start(s32[16,2,192]{2,0,1:T(8,128)S(1)} %collective-permute-done.3), channel_id=1, source_target_pairs={{0,1},{1,2},{2,3},{3,4},{4,5},{5,6},{6,7},{7,8},{8,9},{9,10},{10,1... | collective-permute-start | bytes 73736 | tf_op jit(solution)/shard_map/ppermute | solution.py:17
  71.1 6.8 %collective-permute-start.6 = (s32[16,2,192]{2,0,1:T(8,128)S(1)}, s32[16,2,192]{2,0,1:T(8,128)S(1)}, u32[]{:S(2)}, u32[]{:S(2)}) collective-permute-start(s32[16,2,192]{2,0,1:T(8,128)S(1)} %collective-permute-done.4), channel_id=1, source_target_pairs={{0,15},{1,0},{2,1},{3,2},{4,3},{5,4},{6,5},{7,6},{8,7},{9,8},{10,9... | collective-permute-start | bytes 73736 | tf_op jit(solution)/shard_map/ppermute | solution.py:20
  77.8 6.8 %collective-permute-start.7 = (s32[16,2,192]{2,0,1:T(8,128)S(1)}, s32[16,2,192]{2,0,1:T(8,128)S(1)}, u32[]{:S(2)}, u32[]{:S(2)}) collective-permute-start(s32[16,2,192]{2,0,1:T(8,128)S(1)} %collective-permute-done.5), channel_id=1, source_target_pairs={{0,1},{1,2},{2,3},{3,4},{4,5},{5,6},{6,7},{7,8},{8,9},{9,10},{10,1... | collective-permute-start | bytes 73736 | tf_op jit(solution)/shard_map/ppermute | solution.py:17
  77.9 6.8 %collective-permute-start.8 = (s32[16,2,192]{2,0,1:T(8,128)S(1)}, s32[16,2,192]{2,0,1:T(8,128)S(1)}, u32[]{:S(2)}, u32[]{:S(2)}) collective-permute-start(s32[16,2,192]{2,0,1:T(8,128)S(1)} %collective-permute-done.6), channel_id=1, source_target_pairs={{0,15},{1,0},{2,1},{3,2},{4,3},{5,4},{6,5},{7,6},{8,7},{9,8},{10,9... | collective-permute-start | bytes 73736 | tf_op jit(solution)/shard_map/ppermute | solution.py:20
  84.6 6.8 %collective-permute-start.9 = (s32[16,2,192]{2,0,1:T(8,128)S(1)}, s32[16,2,192]{2,0,1:T(8,128)S(1)}, u32[]{:S(2)}, u32[]{:S(2)}) collective-permute-start(s32[16,2,192]{2,0,1:T(8,128)S(1)} %collective-permute-done.7), channel_id=1, source_target_pairs={{0,1},{1,2},{2,3},{3,4},{4,5},{5,6},{6,7},{7,8},{8,9},{9,10},{10,1... | collective-permute-start | bytes 73736 | tf_op jit(solution)/shard_map/ppermute | solution.py:17
  84.6 6.8 %collective-permute-start.10 = (s32[16,2,192]{2,0,1:T(8,128)S(1)}, s32[16,2,192]{2,0,1:T(8,128)S(1)}, u32[]{:S(2)}, u32[]{:S(2)}) collective-permute-start(s32[16,2,192]{2,0,1:T(8,128)S(1)} %collective-permute-done.8), channel_id=1, source_target_pairs={{0,15},{1,0},{2,1},{3,2},{4,3},{5,4},{6,5},{7,6},{8,7},{9,8},{10,9... | collective-permute-start | bytes 73736 | tf_op jit(solution)/shard_map/ppermute | solution.py:20
  91.4 6.1 %collective-permute-start.11 = (s32[16,2,192]{2,0,1:T(8,128)S(1)}, s32[16,2,192]{2,0,1:T(8,128)S(1)}, u32[]{:S(2)}, u32[]{:S(2)}) collective-permute-start(s32[16,2,192]{2,0,1:T(8,128)S(1)} %collective-permute-done.9), channel_id=1, source_target_pairs={{0,1},{1,2},{2,3},{3,4},{4,5},{5,6},{6,7},{7,8},{8,9},{9,10},{10,1... | collective-permute-start | bytes 73736 | tf_op jit(solution)/shard_map/ppermute | solution.py:17
  91.4 6.1 %collective-permute-start.12 = (s32[16,2,192]{2,0,1:T(8,128)S(1)}, s32[16,2,192]{2,0,1:T(8,128)S(1)}, u32[]{:S(2)}, u32[]{:S(2)}) collective-permute-start(s32[16,2,192]{2,0,1:T(8,128)S(1)} %collective-permute-done.10), channel_id=1, source_target_pairs={{0,15},{1,0},{2,1},{3,2},{4,3},{5,4},{6,5},{7,6},{8,7},{9,8},{10,9... | collective-permute-start | bytes 73736 | tf_op jit(solution)/shard_map/ppermute | solution.py:20
  97.4 6.1 %collective-permute-start.13 = (s32[16,2,192]{2,0,1:T(8,128)S(1)}, s32[16,2,192]{2,0,1:T(8,128)S(1)}, u32[]{:S(2)}, u32[]{:S(2)}) collective-permute-start(s32[16,2,192]{2,0,1:T(8,128)S(1)} %collective-permute-done.11), channel_id=1, source_target_pairs={{0,1},{1,2},{2,3},{3,4},{4,5},{5,6},{6,7},{7,8},{8,9},{9,10},{10,1... | collective-permute-start | bytes 73736 | tf_op jit(solution)/shard_map/ppermute | solution.py:17
  97.5 6.1 %collective-permute-start.14 = (s32[16,2,192]{2,0,1:T(8,128)S(1)}, s32[16,2,192]{2,0,1:T(8,128)S(1)}, u32[]{:S(2)}, u32[]{:S(2)}) collective-permute-start(s32[16,2,192]{2,0,1:T(8,128)S(1)} %collective-permute-done.12), channel_id=1, source_target_pairs={{0,15},{1,0},{2,1},{3,2},{4,3},{5,4},{6,5},{7,6},{8,7},{9,8},{10,9... | collective-permute-start | bytes 73736 | tf_op jit(solution)/shard_map/ppermute | solution.py:20
  103.5 6.1 %collective-permute-start.15 = (s32[16,2,192]{2,0,1:T(8,128)S(1)}, s32[16,2,192]{2,0,1:T(8,128)S(1)}, u32[]{:S(2)}, u32[]{:S(2)}) collective-permute-start(s32[16,2,192]{2,0,1:T(8,128)S(1)} %collective-permute-done.13), channel_id=1, source_target_pairs={{0,1},{1,2},{2,3},{3,4},{4,5},{5,6},{6,7},{7,8},{8,9},{9,10},{10,1... | collective-permute-start | bytes 73736 | tf_op jit(solution)/shard_map/ppermute | solution.py:17
  131.5 19.6 %collective-permute-start.16 = (bf16[16,192,128]{2,1,0:T(8,128)(2,1)S(1)}, bf16[16,192,128]{2,1,0:T(8,128)(2,1)S(1)}, u32[]{:S(2)}, u32[]{:S(2)}) collective-permute-start(bf16[16,192,128]{2,1,0:T(8,128)(2,1)S(1)} %get-tuple-element.32), channel_id=1, source_target_pairs={{16,0},{32,16},{48,32},{64,48},{80,64},{96,80},{112,96},{17,1},{33... | collective-permute-start | bytes 2359304 | tf_op jit(solution)/shard_map/ppermute | solution.py:30
  172.6 1.2 copy-start
  172.6 1.3 copy-start.1
  172.6 1.5 copy-start.4
  175.4 1.4 copy-start.2
  175.4 1.4 copy-start.3
  182.0 8.0 %collective-permute-start.17 = (bf16[4,128,512]{2,1,0:T(8,128)(2,1)S(1)}, bf16[4,128,512]{2,1,0:T(8,128)(2,1)S(1)}, u32[]{:S(2)}, u32[]{:S(2)}) collective-permute-start(bf16[4,128,512]{2,1,0:T(8,128)(2,1)S(1)} %get-tuple-element.21), channel_id=1, source_target_pairs={{0,16},{16,32},{32,48},{48,64},{64,80},{80,96},{96,112},{1,17},{17... | collective-permute-start | bytes 1572872 | tf_op jit(solution)/shard_map/ppermute | solution.py:38
  184.0 10.5 %collective-permute-start.18 = (bf16[4,128,512]{2,1,0:T(8,128)(2,1)S(1)}, bf16[4,128,512]{2,1,0:T(8,128)(2,1)S(1)}, u32[]{:S(2)}, u32[]{:S(2)}) collective-permute-start(bf16[4,128,512]{2,1,0:T(8,128)(2,1)S(1)} %get-tuple-element.22), channel_id=1, source_target_pairs={{16,0},{32,16},{48,32},{64,48},{80,64},{96,80},{112,96},{17,1},{33... | collective-permute-start | bytes 1572872 | tf_op jit(solution)/shard_map/ppermute | solution.py:41
  196.0 18.1 %collective-permute-start.19 = (bf16[4,768,128]{2,1,0:T(8,128)(2,1)}, bf16[4,768,128]{2,1,0:T(8,128)(2,1)}, u32[]{:S(2)}, u32[]{:S(2)}) collective-permute-start(bf16[4,768,128]{2,1,0:T(8,128)(2,1)} %get-tuple-element.13), channel_id=1, source_target_pairs={{0,1},{1,2},{2,3},{3,4},{4,5},{5,6},{6,7},{7,8},{8,9},{9,10},{10,1... | collective-permute-start | bytes 2359304 | tf_op jit(solution)/shard_map/ppermute | solution.py:38
  198.1 20.9 %collective-permute-start.20 = (bf16[4,768,128]{2,1,0:T(8,128)(2,1)}, bf16[4,768,128]{2,1,0:T(8,128)(2,1)}, u32[]{:S(2)}, u32[]{:S(2)}) collective-permute-start(bf16[4,768,128]{2,1,0:T(8,128)(2,1)} %get-tuple-element.14), channel_id=1, source_target_pairs={{1,0},{2,1},{3,2},{4,3},{5,4},{6,5},{7,6},{8,7},{9,8},{10,9},{11,1... | collective-permute-start | bytes 2359304 | tf_op jit(solution)/shard_map/ppermute | solution.py:41
Sparse Core Ops, SparseCore 0:
  9.5 82.7 all-gather.1
